TPU v7x, 32 devices: a whole 2x2x4 slice. The times are simulated.
32 devices in a mesh: seq: 4 (over z), tp: 4 (over y, x), dp: 2 (over core).
Axes of the slice: x: 2, y: 2, z: 4, core: 2. Of those that a mesh axis runs over, the one named last changes fastest.
Arguments:
- hidden_states: bfloat16 [2048, 7168], P(('dp', 'seq'), 'tp'), parts along dimension 0, may hold values from -120 to 120
- input_gain: float32 [7168], P('tp'), may hold values from 0.1 to 1.9
- query_down: bfloat16 [7168, 1536], P('tp', 'seq'), may hold values from -0.0625 to 0.0625
- memory_down: bfloat16 [7168, 576], P('tp', 'seq'), may hold values from -0.0625 to 0.0625
- query_gain: float32 [1536], replicated, may hold values from 0.1 to 1.9
- memory_gain: float32 [512], replicated, may hold values from 0.1 to 1.9
- query_up: bfloat16 [1536, 12288], P('seq', 'tp'), may hold values from -16 to 16
- key_up: bfloat16 [512, 8192], P('seq', 'tp'), may hold values from -0.25 to 0.25
- value_up: bfloat16 [512, 8192], P('seq', 'tp'), may hold values from -0.25 to 0.25
- segment_ids: int32 [2048], P(('dp', 'seq')), parts along dimension 0, may hold values from 0 to 11, never falling along the last dimension, each value on 1 to 256 neighbouring positions
Outputs:
- attended: bfloat16 [2048, 8192], P(('dp', 'seq'), 'tp'), parts along dimension 0
There are 2 independent parts, one for each index of `dp`. A program takes and returns all parts, laid end to end along the dimension named above; an argument that names none is the same for every part. Nothing has to cross between parts.
Inputs may be any that keep to these rules, and one draw needn't show every extreme that they name: `segment_ids`: ids never fall along the group; each of the 12 documents has 1 to 256 tokens and one has exactly 256.
All inputs are finite; a program needn't handle non-finite values.
Results may differ from a plain program's by a relative error of at most 0.0065.
The roundings to bfloat16 on the way count: a program that leaves them out, or rounds other values in their place, can miss the bound.
Values may be sent and summed in bfloat16 or wider, within the bound.
No kernel may reach another device: no remote copies, remote signals or barrier semaphores. Data moves between devices by JAX's collectives and lax.ppermute only.
A program may use at most 128 MiB of HBM per device.

v0:
```python
import jax
import jax.numpy as jnp
from jax import lax
from jax.sharding import PartitionSpec as P

KVRANK = 512
NOPE = 128
ROPE = 64
VDIM = 128
DOCS = 12
epsilon = 1e-06


def rms_scale(entries, gain_vector):
    return (
        entries * lax.rsqrt(jnp.mean(entries * entries, -1, keepdims=True) + epsilon) * gain_vector
    )


def rotate(entries, position):
    half_width = entries.shape[-1] // 2
    frequency = jnp.power(10000.0, -2.0 * jnp.arange(half_width, dtype=jnp.float32) / ROPE)
    angles = position.astype(jnp.float32)[..., None] * frequency
    cosine = jnp.cos(angles)
    sine_part = jnp.sin(angles)
    first_half = entries[..., :half_width]
    second_half = entries[..., half_width:]
    return jnp.concatenate(
        [
            first_half * cosine - second_half * sine_part,
            second_half * cosine + first_half * sine_part,
        ],
        -1,
    )


def heads_attention(query_all, key_all, value_all, group_ids, score_scale, doc_most):
    total_rows = query_all.shape[0]
    block_rows = min(512, total_rows)
    key_index = jnp.arange(total_rows, dtype=jnp.int32)
    results = []
    for block in range(total_rows // block_rows):
        lower = block * block_rows
        upper = lower + block_rows
        key_low = max(0, lower - doc_most)
        scores = (
            jnp.einsum(
                "qhd,khd->hqk",
                query_all[lower:upper],
                key_all[key_low:upper],
                preferred_element_type=jnp.float32,
            )
            * score_scale
        )
        allowed = (group_ids[lower:upper, None] == group_ids[None, key_low:upper]) & (
            key_index[lower:upper, None] >= key_index[None, key_low:upper]
        )
        scores = jnp.where(allowed[None], scores, -jnp.inf)
        row_max = jnp.max(scores, -1, keepdims=True)
        probs_full = jnp.exp(scores - row_max)
        denominator = jnp.sum(probs_full, -1)
        weights = probs_full.astype(jnp.bfloat16)
        weighted = jnp.einsum(
            "hqk,khd->qhd", weights, value_all[key_low:upper], preferred_element_type=jnp.float32
        )
        results.append((weighted / jnp.transpose(denominator)[:, :, None]).astype(jnp.bfloat16))
    return jnp.concatenate(results, 0)


def body(
    hidden_states,
    input_gain,
    query_down,
    memory_down,
    query_gain,
    memory_gain,
    query_up,
    key_up,
    value_up,
    segment_ids,
):
    tok_count = hidden_states.shape[0]
    seq_count = lax.axis_size("seq")
    tp_count = lax.axis_size("tp")
    seq_index = lax.axis_index("seq")
    tp_index = lax.axis_index("tp")
    width = hidden_states.shape[1] * tp_count
    total_rows = tok_count * seq_count
    doc_most = total_rows // 4
    qrank_piece = query_down.shape[1]
    memory_piece = memory_down.shape[1]
    qrank = qrank_piece * seq_count
    memory_cols = memory_piece * seq_count
    group_ids = lax.all_gather(segment_ids, "seq", axis=0, tiled=True)
    token_index = jnp.arange(total_rows, dtype=jnp.int32)
    onehot = group_ids[:, None] == jnp.arange(DOCS, dtype=jnp.int32)[None, :]
    starts = jnp.min(jnp.where(onehot, token_index[:, None], total_rows), 0)
    position = token_index - jnp.sum(jnp.where(onehot, starts[None, :], 0), 1)
    inputs = hidden_states.astype(jnp.float32)
    square_sums = lax.psum(jnp.sum(inputs * inputs, 1), "tp")
    normed = (inputs * lax.rsqrt(square_sums / width + epsilon)[:, None] * input_gain).astype(
        jnp.bfloat16
    )
    down_piece = jnp.concatenate([query_down, memory_down], 1)
    down_all = lax.all_gather(down_piece, "seq", axis=1, tiled=True)
    partial = jnp.dot(normed, down_all, preferred_element_type=jnp.float32)
    latent_rows = lax.psum_scatter(partial, "tp", scatter_dimension=0, tiled=True)
    chunk = latent_rows.shape[0]
    latent_rows = latent_rows.reshape(chunk, seq_count, qrank_piece + memory_piece)
    query_sums = latent_rows[:, :, :qrank_piece].reshape(chunk, qrank)
    memory_sums = latent_rows[:, :, qrank_piece:].reshape(chunk, memory_cols)
    chunk_position = lax.dynamic_slice(
        position, (seq_index * tok_count + tp_index * chunk,), (chunk,)
    )
    compressed_query = rms_scale(query_sums, query_gain).astype(jnp.bfloat16)
    compressed_memory = rms_scale(memory_sums[:, :KVRANK], memory_gain).astype(jnp.bfloat16)
    key_rope = rotate(memory_sums[:, KVRANK:], chunk_position).astype(jnp.bfloat16)
    packed = jnp.concatenate([compressed_query, compressed_memory, key_rope], 1)
    packed = lax.all_gather(packed, "seq", axis=0, tiled=False)
    packed = lax.all_gather(packed, "tp", axis=0, tiled=False)
    latent = jnp.transpose(packed, (1, 0, 2, 3)).reshape(total_rows, packed.shape[-1])
    cq_all = latent[:, :qrank]
    cm_all = latent[:, qrank : qrank + KVRANK]
    rope_all = latent[:, qrank + KVRANK :]
    local_heads = query_up.shape[1] // (NOPE + ROPE)
    heads = local_heads // seq_count
    query_w = lax.all_to_all(
        query_up.reshape(query_up.shape[0], seq_count, heads * (NOPE + ROPE)),
        "seq",
        split_axis=1,
        concat_axis=0,
        tiled=True,
    ).reshape(qrank, heads * (NOPE + ROPE))
    key_w = lax.all_to_all(
        key_up.reshape(key_up.shape[0], seq_count, heads * NOPE),
        "seq",
        split_axis=1,
        concat_axis=0,
        tiled=True,
    ).reshape(KVRANK, heads * NOPE)
    value_w = lax.all_to_all(
        value_up.reshape(value_up.shape[0], seq_count, heads * VDIM),
        "seq",
        split_axis=1,
        concat_axis=0,
        tiled=True,
    ).reshape(KVRANK, heads * VDIM)
    query_full = jnp.dot(cq_all, query_w, preferred_element_type=jnp.float32).reshape(
        total_rows, heads, NOPE + ROPE
    )
    query = jnp.concatenate(
        [query_full[..., :NOPE], rotate(query_full[..., NOPE:], position[:, None])], -1
    ).astype(jnp.bfloat16)
    key_nope = (
        jnp.dot(cm_all, key_w, preferred_element_type=jnp.float32)
        .astype(jnp.bfloat16)
        .reshape(total_rows, heads, NOPE)
    )
    value = (
        jnp.dot(cm_all, value_w, preferred_element_type=jnp.float32)
        .astype(jnp.bfloat16)
        .reshape(total_rows, heads, VDIM)
    )
    key_all = jnp.concatenate(
        [key_nope, jnp.broadcast_to(rope_all[:, None, :], (total_rows, heads, ROPE))], -1
    )
    score_scale = (NOPE + ROPE) ** (-0.5)
    head_output = heads_attention(query, key_all, value, group_ids, score_scale, doc_most)
    attended = lax.all_to_all(head_output, "seq", split_axis=0, concat_axis=1, tiled=True)
    return attended.reshape(tok_count, local_heads * VDIM)


def solution(mesh):
    in_specs = (
        P(("dp", "seq"), "tp"),
        P("tp"),
        P("tp", "seq"),
        P("tp", "seq"),
        P(),
        P(),
        P("seq", "tp"),
        P("seq", "tp"),
        P("seq", "tp"),
        P(("dp", "seq")),
    )
    out_specs = P(("dp", "seq"), "tp")
    return jax.shard_map(body, mesh=mesh, in_specs=in_specs, out_specs=out_specs, check_vma=False)
```

profile of v0, /device:TPU:0, one launch (start us, length us, event | category | flops | bytes accessed | tf_op | source)
XLA Modules:
  0.0 378.8 jit_solution(2457869246093978417)
XLA Ops:
  6.5 1.8 copy.69
  8.4 2.6 pad_maximum_fusion
  11.0 0.0 reduce-scatter.2.cloned.1.call-start
  11.0 0.3 fusion.16
  11.3 11.4 %psum.7 = f32[256]{0:T(256)S(1)} all-reduce(f32[256]{0:T(256)S(1)} %fusion.16), channel_id=1, replica_groups=mesh['seq'=4,'tp'=4,'dp'=2] {'tp'}, use_global_device_ids=true, to_apply=%region_1.2 | all-reduce | flops 256 | bytes 2048 | tf_op jit(solution)/shard_map/psum | solution.py:100
  22.7 127.4 %all-gather.7.cloned.1.call-done = bf16[1792,2112]{0,1:T(8,128)(2,1)} async-done(((bf16[1792,528]{0,1:T(8,128)(2,1)}), bf16[1792,2112]{0,1:T(8,128)(2,1)}) %all-gather.7.cloned.1.call-update) | async-done | bytes 7569424 | tf_op jit(solution)/shard_map/all_gather | solution.py:105
  150.1 6.9 %fusion.33 = f32[256,2112]{1,0:T(8,128)} fusion(bf16[1792,2112]{0,1:T(8,128)(2,1)} %all-gather.7.cloned.1.call-done, bf16[256,1792]{1,0:T(8,128)(2,1)S(1)} %copy-done.5, f32[1792]{0:T(1024)S(1)} %copy-done.14, f32[256]{0:T(256)S(1)} %add_rsqrt_fusion), kind=kOutput, calls=%fused_computation.43 | convolution fusion | flops 1939603456 | bytes 10657792 | tf_op jit(solution)/shard_map/dot_general | solution.py:106
  157.1 7.9 %all-gather.2 = s32[4,1,256]{2,1,0:T(1,128)S(1)} all-gather(s32[1,1,256]{2,1,0:T(1,128)S(1)} %bitcast.83), channel_id=1, replica_groups=mesh['seq'=4,'tp'=4,'dp'=2] {'seq'}, dimensions={0}, use_global_device_ids=true | all-gather | bytes 5120 | tf_op jit(solution)/shard_map/all_gather | solution.py:94
  165.0 0.1 select_reduce_fusion.1
  165.1 0.1 select_reduce_fusion
  165.2 0.1 dynamic-slice_convert_fusion
  165.3 26.4 %reduce-scatter.2.cloned.1.call-done = f32[64,2112]{1,0:T(8,128)} async-done(((f32[256,2112]{1,0:T(8,128)}), f32[64,2112]{1,0:T(8,128)}) %reduce-scatter.2.cloned.1.call-update) | async-done | bytes 540688 | tf_op jit(solution)/shard_map/reduce_scatter | solution.py:107
  191.7 1.5 reshape.261
  193.2 0.6 multiply_reduce_fusion
  193.8 0.2 copy.87
  193.9 0.1 multiply_reduce_fusion.1
  194.0 0.1 fusion.49
  194.2 0.1 copy.72
  194.3 0.1 copy.73
  194.4 0.1 multiply_convert_fusion.1
  194.5 0.1 copy.71
  194.7 0.1 multiply_convert_fusion
  194.8 0.8 concatenate.20
  195.7 29.2 %all-gather.9.cloned.1.call-done = bf16[256,2112]{1,0:T(8,128)(2,1)} async-done(((bf16[64,2112]{1,0:T(8,128)(2,1)}), bf16[256,2112]{1,0:T(8,128)(2,1)}) %all-gather.9.cloned.1.call-update) | async-done | bytes 1081360 | tf_op jit(solution)/shard_map/all_gather | solution.py:119
  224.9 1.0 copy.80
  225.9 3.5 all-to-all-start.2
  229.4 1.0 copy.75
  230.4 13.3 %all-to-all-done.2 = bf16[128,4,512]{0,2,1:T(8,128)(2,1)S(1)} async-done(((bf16[128,4,512]{0,2,1:T(8,128)(2,1)}), bf16[128,4,512]{0,2,1:T(8,128)(2,1)S(1)}, u32[]{:S(2)}, u32[]{:S(2)}) %all-to-all-start.2) | async-done | bytes 524320 | tf_op jit(solution)/shard_map/all_to_all | solution.py:134
  243.7 3.5 all-to-all-start
  247.1 3.0 copy.77
  250.2 2.7 copy.78
  252.8 8.3 %all-to-all-done = bf16[128,4,512]{0,2,1:T(8,128)(2,1)S(1)} async-done(((bf16[128,4,512]{0,2,1:T(8,128)(2,1)}), bf16[128,4,512]{0,2,1:T(8,128)(2,1)S(1)}, u32[]{:S(2)}, u32[]{:S(2)}) %all-to-all-start) | async-done | bytes 524320 | tf_op jit(solution)/shard_map/all_to_all | solution.py:141
  261.2 3.8 %all-to-all-start.1 = ((bf16[384,4,768]{2,0,1:T(8,128)(2,1)}), bf16[384,4,768]{2,0,1:T(8,128)(2,1)S(1)}, u32[]{:S(2)}, u32[]{:S(2)}) async-start(bf16[384,4,768]{2,0,1:T(8,128)(2,1)} %copy.78), calls=%async_computation.2 | async-start | bytes 4718592 | tf_op jit(solution)/shard_map/all_to_all | solution.py:127
  265.0 0.6 slice.105
  265.6 1.8 multiply_cosine_fusion
  267.4 1.0 compare_and_fusion.1
  268.4 1.8 compare_and_fusion
  270.3 1.0 copy.81
  271.3 0.2 copy.76
  271.5 46.6 %all-to-all-done.1 = bf16[384,4,768]{2,0,1:T(8,128)(2,1)S(1)} async-done(((bf16[384,4,768]{2,0,1:T(8,128)(2,1)}), bf16[384,4,768]{2,0,1:T(8,128)(2,1)S(1)}, u32[]{:S(2)}, u32[]{:S(2)}) %all-to-all-start.1) | async-done | bytes 2359328 | tf_op jit(solution)/shard_map/all_to_all | solution.py:127
  318.1 2.4 copy.79
  320.6 2.6 copy.74
  323.2 0.8 convolution_convert_fusion.1
  324.0 0.8 copy-done
  324.9 2.6 fusion.6
  327.5 0.2 slice.163
  327.7 1.5 copy-done.3
  329.1 1.8 convolution_convert_fusion
  330.9 0.1 copy.82
  331.1 1.4 subtract_convert_fusion
  332.5 0.2 pad_maximum_fusion.1
  332.7 0.1 broadcast_in_dim.51
  332.8 1.0 fusion.3
  333.8 1.7 fusion
  335.5 0.9 fusion.4
  336.4 0.1 slice-done
  336.6 1.3 divide_convert_fusion.1
  337.9 1.7 fusion.1
  339.6 2.1 divide_convert_fusion
  341.7 0.1 pad_maximum_fusion.4
  341.8 0.8 copy.84
  342.6 27.7 %all_to_all.60 = bf16[1024,4,128]{2,1,0:T(4,128)(2,1)S(1)} all-to-all(bf16[1024,4,128]{2,1,0:T(4,128)(2,1)S(1)} %copy.84), channel_id=1, replica_groups=mesh['seq'=4,'tp'=4,'dp'=2] {'seq'}, dimensions={0} | all-to-all | bytes 2097152 | tf_op jit(solution)/shard_map/all_to_all | solution.py:169
  370.3 0.4 copy.85
  370.6 1.6 reshape.272
  (56 shorter events, 0.4 us)
Async XLA Ops:
  6.5 143.5 %all-gather.7.cloned.1.call-start = ((), (), s32[]{:S(2)}) async-start(), calls=%async_computation.5 | async-start | bytes 9461760 | tf_op jit(solution)/shard_map/all_gather | solution.py:105
  8.3 2.7 copy-start.5
  8.4 141.7 %copy-start.14 = (f32[1792]{0:T(1024)S(1)}, f32[1792]{0:T(1024)}, u32[]{:S(2)}) copy-start(f32[1792]{0:T(1024)} %param.11) | copy-start | bytes 21508
  11.0 180.7 %reduce-scatter.2.cloned.1.call-start = ((), (), s32[]{:S(2)}) async-start(), calls=%async_computation.6 | async-start | bytes 2785280 | tf_op jit(solution)/shard_map/reduce_scatter | solution.py:107
  22.7 134.4 %copy-start.13 = (s32[256]{0:T(256)S(1)}, s32[256]{0:T(256)}, u32[]{:S(2)}) copy-start(s32[256]{0:T(256)} %param.19) | copy-start | bytes 3076
  157.0 37.4 %copy-start.11 = (f32[512]{0:T(512)S(1)}, f32[512]{0:T(512)}, u32[]{:S(2)}) copy-start(f32[512]{0:T(512)} %param.15) | copy-start | bytes 6148
  157.0 37.7 %copy-start.10 = (f32[1536]{0:T(1024)S(1)}, f32[1536]{0:T(1024)}, u32[]{:S(2)}) copy-start(f32[1536]{0:T(1024)} %param.14) | copy-start | bytes 18436
  157.0 67.8 %all-gather.9.cloned.1.call-start = ((), (), s32[]{:S(2)}) async-start(), calls=%async_computation.7 | async-start | bytes 1392640 | tf_op jit(solution)/shard_map/all_gather | solution.py:119
  165.0 30.7 %copy-start.12 = (f32[32]{0:T(128)}, f32[32]{0:T(128)S(1)}, u32[]{:S(2)}) copy-start(f32[32]{0:T(128)S(1)} %multiply_power_fusion) | copy-start | bytes 388
  193.2 31.8 %copy-start.7 = (bf16[128,2048]{1,0:T(8,128)(2,1)S(1)}, bf16[128,2048]{1,0:T(8,128)(2,1)}, u32[]{:S(2)}) copy-start(bf16[128,2048]{1,0:T(8,128)(2,1)} %param.17) | copy-start | bytes 1572868
  194.0 35.4 %copy-start.8 = (bf16[128,2048]{1,0:T(8,128)(2,1)S(1)}, bf16[128,2048]{1,0:T(8,128)(2,1)}, u32[]{:S(2)}) copy-start(bf16[128,2048]{1,0:T(8,128)(2,1)} %param.18) | copy-start | bytes 1572868
  195.7 124.9 %all-gather.11.cloned.1.call-start = ((), (), s32[]{:S(2)}) async-start(), calls=%async_computation.8 | async-start | bytes 5570560 | tf_op jit(solution)/shard_map/all_gather | solution.py:120
  225.9 17.7 %all-to-all-start.2 = ((bf16[128,4,512]{0,2,1:T(8,128)(2,1)}), bf16[128,4,512]{0,2,1:T(8,128)(2,1)S(1)}, u32[]{:S(2)}, u32[]{:S(2)}) async-start(bf16[128,4,512]{0,2,1:T(8,128)(2,1)} %bitcast.20), calls=%async_computation.3 | async-start | bytes 1048576 | tf_op jit(solution)/shard_map/all_to_all | solution.py:134
  243.7 17.5 %all-to-all-start = ((bf16[128,4,512]{0,2,1:T(8,128)(2,1)}), bf16[128,4,512]{0,2,1:T(8,128)(2,1)S(1)}, u32[]{:S(2)}, u32[]{:S(2)}) async-start(bf16[128,4,512]{0,2,1:T(8,128)(2,1)} %bitcast.7), calls=%async_computation.1 | async-start | bytes 1048576 | tf_op jit(solution)/shard_map/all_to_all | solution.py:141
  261.2 57.0 %all-to-all-start.1 = ((bf16[384,4,768]{2,0,1:T(8,128)(2,1)}), bf16[384,4,768]{2,0,1:T(8,128)(2,1)S(1)}, u32[]{:S(2)}, u32[]{:S(2)}) async-start(bf16[384,4,768]{2,0,1:T(8,128)(2,1)} %copy.78), calls=%async_computation.2 | async-start | bytes 4718592 | tf_op jit(solution)/shard_map/all_to_all | solution.py:127
  323.2 1.7 copy-start
  324.0 3.5 copy-start.1
  324.9 4.3 %copy-start.9 = (bf16[4,128,1,512]{3,1,0,2:T(8,128)(2,1)S(1)}, bf16[4,128,1,512]{3,1,0,2:T(8,128)(2,1)}, u32[]{:S(2)}) copy-start(bf16[4,128,1,512]{3,1,0,2:T(8,128)(2,1)} %copy.81) | copy-start | bytes 1572868
  327.5 1.6 copy-start.3
  327.5 3.5 copy-start.6
  330.9 1.8 copy-start.4
  331.0 1.7 copy-start.15
  332.8 1.0 copy-start.2
  335.5 1.0 slice-start
  337.9 1.7 slice-start.1
Sparse Core Ops, SparseCore 0:
  11.1 138.9 all-gather.6
  157.2 34.4 reduce-scatter.1
  195.8 29.0 all-gather.8
  226.6 54.1 all-gather.10
where the time goes:
time: 380 us; the launch traced here: 379 us
  waiting for transfers between devices  251 us (66%)
  blocking collectives  46.9 us (12%)
  local copies, waits for them, and re-layouts  24.8 us (7%)
  matrix products  18.2 us (5%)
  between operations  13.6 us (4%)
  other arithmetic  13.2 us (3%)
  starting transfers between devices  10.9 us (3%)
    all_gather x1, waiting for transfers between devices, body(): down_all = lax.all_gather(down_piece, 'seq', axis=1, tiled=True)  127 us
    all_to_all x1, waiting for transfers between devices, body(): lax.all_to_all(query_up.reshape(query_up.shape[0], seq_count, heads * (NO...  46.6 us
    all_gather x1, waiting for transfers between devices, body(): packed = lax.all_gather(packed, 'seq', axis=0, tiled=False)  29.2 us
    all_to_all x1, blocking collectives, body(): lax.all_to_all(head_output, 'seq', split_axis=0, concat_axis=1, tiled=True)  27.7 us
    reduce_scatter x1, waiting for transfers between devices, body(): lax.psum_scatter(partial, 'tp', scatter_dimension=0, tiled=True)  26.4 us
    all_to_all x1, waiting for transfers between devices, body(): lax.all_to_all(key_up.reshape(key_up.shape[0], seq_count, heads * NOPE),...  13.3 us
    psum x1, blocking collectives, body(): square_sums = lax.psum(jnp.sum(inputs * inputs, 1), 'tp')  11.4 us
    unnamed x38, local copies, waits for them, and re-layouts  9.38 us
  transfers between devices with their start and end apart: 7, of which 6 were waited for; matrix products, arithmetic and copies ran while one was open for 5% of the time, Pallas kernels for 0%

commit v1 on v0

--- a/solution.py
+++ b/solution.py
@@ -9,6 +9,22 @@
 VDIM = 128
 DOCS = 12
 epsilon = 1e-06
+
+
+def pairwise_exchange(array, axis, split, join):
+    ways, here = (lax.axis_size(axis), lax.axis_index(axis))
+    width = array.shape[split] // ways
+    dims = list(array.shape)
+    dims[split] = width
+    height = dims[join]
+    dims[join] = height * ways
+    full = jnp.zeros(dims, array.dtype)
+    for mask in range(ways):
+        part = lax.dynamic_slice_in_dim(array, (here ^ mask) * width, width, axis=split)
+        if mask:
+            part = lax.ppermute(part, axis, [(d, d ^ mask) for d in range(ways)])
+        full = lax.dynamic_update_slice_in_dim(full, part, (here ^ mask) * height, axis=join)
+    return full
 
 
 def rms_scale(entries, gain_vector):
@@ -166,7 +182,7 @@
     )
     score_scale = (NOPE + ROPE) ** (-0.5)
     head_output = heads_attention(query, key_all, value, group_ids, score_scale, doc_most)
-    attended = lax.all_to_all(head_output, "seq", split_axis=0, concat_axis=1, tiled=True)
+    attended = pairwise_exchange(head_output, "seq", 0, 1)
     return attended.reshape(tok_count, local_heads * VDIM)
 
 

time: 380 us -> 376 us (0.989)
  blocking collectives: 46.9 us -> 19.2 us
  waiting for transfers between devices: 251 us -> 267 us
  starting transfers between devices: 10.9 us -> 15.3 us
    all_to_all x1 -> x0, blocking collectives: 27.7 us -> none  [body(): lax.all_to_all(head_output, 'seq', split_axis=0, concat_axis=1, tiled=True)]
    ppermute x0 -> x3, waiting for transfers between devices: none -> 16.8 us  [pairwise_exchange(): part = lax.ppermute(part, axis, [(d, d ^ mask) for d in range(ways)])]
    all_to_all x1, waiting for transfers between devices: 13.3 us -> 8.32 us  [body(): lax.all_to_all(key_up.reshape(key_up.shape[0], seq_count, heads * NOPE),...]
    all_to_all x1, waiting for transfers between devices: 8.31 us -> 13.2 us  [body(): lax.all_to_all(value_up.reshape(value_up.shape[0], seq_count, heads * VDI...]
    ppermute x0 -> x3, starting transfers between devices: none -> 4.44 us  [pairwise_exchange(): part = lax.ppermute(part, axis, [(d, d ^ mask) for d in range(ways)])]
    unnamed x38 -> x43, local copies, waits for them, and re-layouts: 9.38 us -> 9.89 us
  transfers between devices with their start and end apart: 7 -> 10, of which waited for: 6 -> 8; matrix products, arithmetic and copies ran while one was open for 5% -> 5% of each run, Pallas kernels for 0% -> 0%
where the time goes in v1:
time: 376 us; the launch traced here: 375 us
  waiting for transfers between devices  267 us (71%)
  local copies, waits for them, and re-layouts  27.4 us (7%)
  matrix products  20.3 us (5%)
  blocking collectives  19.2 us (5%)
  starting transfers between devices  15.3 us (4%)
  between operations  13.6 us (4%)
  other arithmetic  12.2 us (3%)
    all_gather x1, waiting for transfers between devices, body(): down_all = lax.all_gather(down_piece, 'seq', axis=1, tiled=True)  127 us
    all_to_all x1, waiting for transfers between devices, body(): lax.all_to_all(query_up.reshape(query_up.shape[0], seq_count, heads * (NO...  45.8 us
    all_gather x1, waiting for transfers between devices, body(): packed = lax.all_gather(packed, 'seq', axis=0, tiled=False)  29.2 us
    reduce_scatter x1, waiting for transfers between devices, body(): lax.psum_scatter(partial, 'tp', scatter_dimension=0, tiled=True)  26.4 us
    ppermute x3, waiting for transfers between devices, pairwise_exchange(): part = lax.ppermute(part, axis, [(d, d ^ mask) for d in range(ways)])  16.8 us
    all_to_all x1, waiting for transfers between devices, body(): lax.all_to_all(value_up.reshape(value_up.shape[0], seq_count, heads * VDI...  13.2 us
    psum x1, blocking collectives, body(): square_sums = lax.psum(jnp.sum(inputs * inputs, 1), 'tp')  11.4 us
    unnamed x43, local copies, waits for them, and re-layouts  9.89 us
  transfers between devices with their start and end apart: 10, of which 8 were waited for; matrix products, arithmetic and copies ran while one was open for 5% of the time, Pallas kernels for 0%

profile of v1, /device:TPU:0, one launch (start us, length us, event | category | flops | bytes accessed | tf_op | source)
XLA Modules:
  0.0 375.2 jit_solution(16413752873503942649)
XLA Ops:
  6.5 1.8 copy.72
  8.4 2.6 pad_maximum_fusion
  11.0 0.3 fusion.16
  11.3 11.4 %psum.7 = f32[256]{0:T(256)S(1)} all-reduce(f32[256]{0:T(256)S(1)} %fusion.16), channel_id=1, replica_groups=mesh['seq'=4,'tp'=4,'dp'=2] {'tp'}, use_global_device_ids=true, to_apply=%region_1.2 | all-reduce | flops 256 | bytes 2048 | tf_op jit(solution)/shard_map/psum | solution.py:116
  22.7 127.4 %all-gather.7.cloned.1.call-done = bf16[1792,2112]{0,1:T(8,128)(2,1)} async-done(((bf16[1792,528]{0,1:T(8,128)(2,1)}), bf16[1792,2112]{0,1:T(8,128)(2,1)}) %all-gather.7.cloned.1.call-update) | async-done | bytes 7569424 | tf_op jit(solution)/shard_map/all_gather | solution.py:121
  150.1 6.9 %fusion.33 = f32[256,2112]{1,0:T(8,128)} fusion(bf16[1792,2112]{0,1:T(8,128)(2,1)} %all-gather.7.cloned.1.call-done, bf16[256,1792]{1,0:T(8,128)(2,1)S(1)} %copy-done.5, f32[1792]{0:T(1024)S(1)} %copy-done.16, f32[256]{0:T(256)S(1)} %add_rsqrt_fusion), kind=kOutput, calls=%fused_computation.51 | convolution fusion | flops 1939603456 | bytes 10657792 | tf_op jit(solution)/shard_map/dot_general | solution.py:122
  157.1 7.9 %all-gather.2 = s32[4,1,256]{2,1,0:T(1,128)S(1)} all-gather(s32[1,1,256]{2,1,0:T(1,128)S(1)} %bitcast.84), channel_id=1, replica_groups=mesh['seq'=4,'tp'=4,'dp'=2] {'seq'}, dimensions={0}, use_global_device_ids=true | all-gather | bytes 5120 | tf_op jit(solution)/shard_map/all_gather | solution.py:110
  165.0 0.1 select_reduce_fusion.1
  165.3 26.4 %reduce-scatter.2.cloned.1.call-done = f32[64,2112]{1,0:T(8,128)} async-done(((f32[256,2112]{1,0:T(8,128)}), f32[64,2112]{1,0:T(8,128)}) %reduce-scatter.2.cloned.1.call-update) | async-done | bytes 540688 | tf_op jit(solution)/shard_map/reduce_scatter | solution.py:123
  191.7 1.5 reshape.260
  193.2 0.6 multiply_reduce_fusion
  193.8 0.2 copy.90
  194.1 0.1 multiply_convert_fusion.1
  194.2 0.1 copy.74
  194.3 0.1 fusion.54
  194.7 0.1 multiply_convert_fusion
  194.8 0.8 concatenate.20
  195.7 29.2 %all-gather.9.cloned.1.call-done = bf16[256,2112]{1,0:T(8,128)(2,1)} async-done(((bf16[64,2112]{1,0:T(8,128)(2,1)}), bf16[256,2112]{1,0:T(8,128)(2,1)}) %all-gather.9.cloned.1.call-update) | async-done | bytes 1081360 | tf_op jit(solution)/shard_map/all_gather | solution.py:135
  224.9 1.0 copy.78
  225.9 3.5 all-to-all-start
  229.4 1.0 copy.83
  230.4 13.2 %all-to-all-done = bf16[128,4,512]{0,2,1:T(8,128)(2,1)S(1)} async-done(((bf16[128,4,512]{0,2,1:T(8,128)(2,1)}), bf16[128,4,512]{0,2,1:T(8,128)(2,1)S(1)}, u32[]{:S(2)}, u32[]{:S(2)}) %all-to-all-start) | async-done | bytes 524320 | tf_op jit(solution)/shard_map/all_to_all | solution.py:157
  243.7 3.5 all-to-all-start.2
  247.1 3.0 copy.80
  250.1 2.7 copy.81
  252.8 8.3 %all-to-all-done.2 = bf16[128,4,512]{0,2,1:T(8,128)(2,1)S(1)} async-done(((bf16[128,4,512]{0,2,1:T(8,128)(2,1)}), bf16[128,4,512]{0,2,1:T(8,128)(2,1)S(1)}, u32[]{:S(2)}, u32[]{:S(2)}) %all-to-all-start.2) | async-done | bytes 524320 | tf_op jit(solution)/shard_map/all_to_all | solution.py:150
  261.1 3.8 %all-to-all-start.1 = ((bf16[384,4,768]{2,0,1:T(8,128)(2,1)}), bf16[384,4,768]{2,0,1:T(8,128)(2,1)S(1)}, u32[]{:S(2)}, u32[]{:S(2)}) async-start(bf16[384,4,768]{2,0,1:T(8,128)(2,1)} %copy.81), calls=%async_computation.2 | async-start | bytes 4718592 | tf_op jit(solution)/shard_map/all_to_all | solution.py:143
  265.0 0.6 slice.105
  265.6 1.8 multiply_cosine_fusion
  267.5 1.0 compare_and_fusion.1
  268.4 1.8 compare_and_fusion
  270.3 1.0 copy.79
  271.3 1.0 copy.84
  272.3 45.8 %all-to-all-done.1 = bf16[384,4,768]{2,0,1:T(8,128)(2,1)S(1)} async-done(((bf16[384,4,768]{2,0,1:T(8,128)(2,1)}), bf16[384,4,768]{2,0,1:T(8,128)(2,1)S(1)}, u32[]{:S(2)}, u32[]{:S(2)}) %all-to-all-start.1) | async-done | bytes 2359328 | tf_op jit(solution)/shard_map/all_to_all | solution.py:143
  318.1 2.5 copy.82
  320.6 2.7 copy.77
  323.3 0.7 slice.125
  324.0 0.8 convolution_convert_fusion.1
  324.8 0.6 copy-done
  325.4 1.7 convolution_convert_fusion
  327.1 1.7 copy.85
  328.9 4.5 %fusion.6 = f32[1024,4,192]{0,2,1:T(8,128)S(1)} fusion(bf16[4,192,1536]{2,1,0:T(8,128)(2,1)S(1)} %bitcast.68, bf16[1024,2112]{1,0:T(8,128)(2,1)} %bitcast.62), kind=kOutput, calls=%fused_computation.11 | convolution fusion | flops 2415919104 | bytes 8650752 | tf_op jit(solution)/shard_map/dot_general | solution.py:164
  333.4 0.2 slice.163
  333.6 0.2 subtract_convert_fusion
  333.8 0.1 pad_maximum_fusion.1
  333.9 0.4 copy-done.7
  334.4 0.2 copy-done.4
  334.6 0.4 copy-done.17
  334.9 1.0 fusion.3
  336.0 1.7 fusion
  337.7 0.9 fusion.4
  338.6 0.1 slice-done
  338.7 1.3 divide_convert_fusion.1
  340.1 1.7 fusion.1
  341.8 2.3 divide_convert_fusion
  344.2 0.5 fusion.42
  344.7 2.0 collective-permute-start.1
  346.7 2.4 collective-permute-start.2
  349.1 7.9 %collective-permute-done = bf16[256,4,128]{0,2,1:T(8,128)(2,1)S(1)} collective-permute-done((bf16[256,4,128]{0,2,1:T(8,128)(2,1)S(1)}, bf16[256,4,128]{0,2,1:T(8,128)(2,1)S(1)}, u32[]{:S(2)}, u32[]{:S(2)}) %collective-permute-start) | collective-permute-done | bytes 262176 | tf_op jit(solution)/shard_map/ppermute | solution.py:25
  357.0 8.9 %collective-permute-done.1 = bf16[256,4,128]{0,2,1:T(8,128)(2,1)S(1)} collective-permute-done((bf16[256,4,128]{0,2,1:T(8,128)(2,1)S(1)}, bf16[256,4,128]{0,2,1:T(8,128)(2,1)S(1)}, u32[]{:S(2)}, u32[]{:S(2)}) %collective-permute-start.1) | collective-permute-done | bytes 262176 | tf_op jit(solution)/shard_map/ppermute | solution.py:25
  366.0 1.1 copy.87
  367.1 0.2 copy.88
  367.2 0.2 constant_dynamic-update-slice_fusion.2
  367.4 1.2 copy.94
  (69 shorter events, 1.1 us)
Async XLA Ops:
  6.5 143.5 %all-gather.7.cloned.1.call-start = ((), (), s32[]{:S(2)}) async-start(), calls=%async_computation.4 | async-start | bytes 9461760 | tf_op jit(solution)/shard_map/all_gather | solution.py:121
  8.3 2.7 copy-start.5
  8.4 141.7 %copy-start.16 = (f32[1792]{0:T(1024)S(1)}, f32[1792]{0:T(1024)}, u32[]{:S(2)}) copy-start(f32[1792]{0:T(1024)} %param.11) | copy-start | bytes 21508
  11.0 180.7 %reduce-scatter.2.cloned.1.call-start = ((), (), s32[]{:S(2)}) async-start(), calls=%async_computation.5 | async-start | bytes 2785280 | tf_op jit(solution)/shard_map/reduce_scatter | solution.py:123
  22.7 134.4 %copy-start.15 = (s32[256]{0:T(256)S(1)}, s32[256]{0:T(256)}, u32[]{:S(2)}) copy-start(s32[256]{0:T(256)} %param.19) | copy-start | bytes 3076
  157.0 37.1 %copy-start.13 = (f32[512]{0:T(512)S(1)}, f32[512]{0:T(512)}, u32[]{:S(2)}) copy-start(f32[512]{0:T(512)} %param.15) | copy-start | bytes 6148
  157.0 37.7 %copy-start.12 = (f32[1536]{0:T(1024)S(1)}, f32[1536]{0:T(1024)}, u32[]{:S(2)}) copy-start(f32[1536]{0:T(1024)} %param.14) | copy-start | bytes 18436
  157.0 67.8 %all-gather.9.cloned.1.call-start = ((), (), s32[]{:S(2)}) async-start(), calls=%async_computation.6 | async-start | bytes 1392640 | tf_op jit(solution)/shard_map/all_gather | solution.py:135
  165.0 30.7 %copy-start.14 = (f32[32]{0:T(128)}, f32[32]{0:T(128)S(1)}, u32[]{:S(2)}) copy-start(f32[32]{0:T(128)S(1)} %multiply_power_fusion) | copy-start | bytes 388
  193.2 31.7 %copy-start.8 = (bf16[128,2048]{1,0:T(8,128)(2,1)S(1)}, bf16[128,2048]{1,0:T(8,128)(2,1)}, u32[]{:S(2)}) copy-start(bf16[128,2048]{1,0:T(8,128)(2,1)} %param.18) | copy-start | bytes 1572868
  193.8 35.6 %copy-start.9 = (bf16[128,2048]{1,0:T(8,128)(2,1)S(1)}, bf16[128,2048]{1,0:T(8,128)(2,1)}, u32[]{:S(2)}) copy-start(bf16[128,2048]{1,0:T(8,128)(2,1)} %param.17) | copy-start | bytes 1572868
  195.7 124.9 %all-gather.11.cloned.1.call-start = ((), (), s32[]{:S(2)}) async-start(), calls=%async_computation.7 | async-start | bytes 5570560 | tf_op jit(solution)/shard_map/all_gather | solution.py:136
  225.9 17.7 %all-to-all-start = ((bf16[128,4,512]{0,2,1:T(8,128)(2,1)}), bf16[128,4,512]{0,2,1:T(8,128)(2,1)S(1)}, u32[]{:S(2)}, u32[]{:S(2)}) async-start(bf16[128,4,512]{0,2,1:T(8,128)(2,1)} %bitcast.7), calls=%async_computation.1 | async-start | bytes 1048576 | tf_op jit(solution)/shard_map/all_to_all | solution.py:157
  243.7 17.5 %all-to-all-start.2 = ((bf16[128,4,512]{0,2,1:T(8,128)(2,1)}), bf16[128,4,512]{0,2,1:T(8,128)(2,1)S(1)}, u32[]{:S(2)}, u32[]{:S(2)}) async-start(bf16[128,4,512]{0,2,1:T(8,128)(2,1)} %bitcast.20), calls=%async_computation.3 | async-start | bytes 1048576 | tf_op jit(solution)/shard_map/all_to_all | solution.py:150
  261.1 57.0 %all-to-all-start.1 = ((bf16[384,4,768]{2,0,1:T(8,128)(2,1)}), bf16[384,4,768]{2,0,1:T(8,128)(2,1)S(1)}, u32[]{:S(2)}, u32[]{:S(2)}) async-start(bf16[384,4,768]{2,0,1:T(8,128)(2,1)} %copy.81), calls=%async_computation.2 | async-start | bytes 4718592 | tf_op jit(solution)/shard_map/all_to_all | solution.py:143
  320.6 3.5 copy-start.11
  323.3 2.1 copy-start
  323.3 2.1 copy-start.10
  324.8 8.6 %copy-start.2 = (bf16[1024,512]{0,1:T(8,128)(2,1)}, bf16[1024,512]{0,1:T(8,128)(2,1)S(1)}, u32[]{:S(2)}) copy-start(bf16[1024,512]{0,1:T(8,128)(2,1)S(1)} %convolution_convert_fusion.1) | copy-start | bytes 3145732
  324.8 4.1 %copy-start.1 = (bf16[1536,768]{0,1:T(8,128)(2,1)S(1)}, bf16[1536,768]{0,1:T(8,128)(2,1)}, u32[]{:S(2)}) copy-start(bf16[1536,768]{0,1:T(8,128)(2,1)} %copy.82) | copy-start | bytes 7077892
  328.9 4.8 %copy-start.6 = (f32[1024,32]{0,1:T(8,128)S(1)}, f32[1024,32]{0,1:T(8,128)}, u32[]{:S(2)}) copy-start(f32[1024,32]{0,1:T(8,128)} %get-tuple-element.16) | copy-start | bytes 393220
  333.4 0.9 copy-start.7
  333.6 1.0 copy-start.4
  333.6 1.3 copy-start.17
  334.9 1.0 copy-start.3
  337.7 1.0 slice-start
  340.0 1.7 slice-start.1
  344.7 12.3 %collective-permute-start = (bf16[256,4,128]{0,2,1:T(8,128)(2,1)S(1)}, bf16[256,4,128]{0,2,1:T(8,128)(2,1)S(1)}, u32[]{:S(2)}, u32[]{:S(2)}) collective-permute-start(bf16[256,4,128]{0,2,1:T(8,128)(2,1)S(1)} %get-tuple-element.9), channel_id=1, source_target_pairs={{0,8},{8,0},{16,24},{24,16},{1,9},{9,1},{17,25},{25,17},{2,10},{10... | collective-permute-start | bytes 786440 | tf_op jit(solution)/shard_map/ppermute | solution.py:25
  344.7 21.2 %collective-permute-start.1 = (bf16[256,4,128]{0,2,1:T(8,128)(2,1)S(1)}, bf16[256,4,128]{0,2,1:T(8,128)(2,1)S(1)}, u32[]{:S(2)}, u32[]{:S(2)}) collective-permute-start(bf16[256,4,128]{0,2,1:T(8,128)(2,1)S(1)} %get-tuple-element.10), channel_id=1, source_target_pairs={{0,16},{8,24},{16,0},{24,8},{1,17},{9,25},{17,1},{25,9},{2,18},{10... | collective-permute-start | bytes 786440 | tf_op jit(solution)/shard_map/ppermute | solution.py:25
  346.7 20.3 %collective-permute-start.2 = (bf16[256,4,128]{0,2,1:T(8,128)(2,1)S(1)}, bf16[256,4,128]{0,2,1:T(8,128)(2,1)S(1)}, u32[]{:S(2)}, u32[]{:S(2)}) collective-permute-start(bf16[256,4,128]{0,2,1:T(8,128)(2,1)S(1)} %get-tuple-element.7), channel_id=1, source_target_pairs={{0,24},{8,16},{16,8},{24,0},{1,25},{9,17},{17,9},{25,1},{2,26},{10... | collective-permute-start | bytes 786440 | tf_op jit(solution)/shard_map/ppermute | solution.py:25
Sparse Core Ops, SparseCore 0:
  11.1 138.9 all-gather.6
  157.2 34.4 reduce-scatter.1
  195.8 29.0 all-gather.8
  226.6 54.1 all-gather.10
